TPU v7x, 32 devices: a whole 2x2x4 slice. The times are simulated.
32 devices in a mesh: clips: 2 (over y), frame: 4 (over x, core), row: 4 (over z).
Axes of the slice: x: 2, y: 2, z: 4, core: 2. Of those that a mesh axis runs over, the one named last changes fastest.
Arguments:
- frames: bfloat16 [16, 512, 640], P(('clips', 'frame'), 'row'), parts along dimension 0, may hold values from -16 to 16
- key_index: int32 [4], P('clips'), parts along dimension 0, may hold values from 0 to 7, as said below
- w_query: bfloat16 [640, 640], replicated, may hold values from -0.25 to 0.25
- w_keyval: bfloat16 [640, 1280], replicated, may hold values from -0.25 to 0.25
- w_out: bfloat16 [640, 640], replicated, may hold values from -0.25 to 0.25
- norm_gain: float32 [640], replicated, may hold values from 0.1 to 1.9
- w_first: bfloat16 [3, 640, 640], replicated, may hold values from -0.125 to 0.125
- w_second: bfloat16 [3, 640, 640], replicated, may hold values from -0.125 to 0.125
Outputs:
- edited: bfloat16 [16, 512, 640], P(('clips', 'frame'), 'row'), parts along dimension 0
There are 2 independent parts, one for each index of `clips`. A program takes and returns all parts, laid end to end along the dimension named above; an argument that names none is the same for every part. Nothing has to cross between parts.
Inputs may be any that keep to these rules, and one draw needn't show every extreme that they name: `key_index`: two different frame indices of the window, in either order; one of them is the window's last frame 8 - 1.
All inputs are finite; a program needn't handle non-finite values.
Results may differ from a plain program's by a relative error of at most 0.0067.
Values may be sent and summed in bfloat16 or wider, within the bound.
No kernel may reach another device: no remote copies, remote signals or barrier semaphores. Data moves between devices by JAX's collectives and lax.ppermute only.
A program may use at most 128 MiB of HBM per device.

v0:
```python
from functools import partial
import jax
import jax.numpy as jnp
from jax import lax
from jax.sharding import PartitionSpec as P

HEADS = 10
HEAD_DIM = 64


def from_root(value, axis, source):
    kept = jnp.where(lax.axis_index(axis) == source, value, 0).astype(value.dtype)
    return lax.psum(kept, axis)


def extended(array, sides, width):
    for axis, dim in sides:
        size, length = (lax.axis_size(axis), array.shape[dim])
        up = [(i, (i + 1) % size) for i in range(size - 1)]
        down = [(j, i) for i, j in up]
        last = lax.slice_in_dim(array, length - width, length, axis=dim)
        first = lax.slice_in_dim(array, 0, width, axis=dim)
        before = lax.ppermute(last, axis, up)
        after = lax.ppermute(first, axis, down)
        array = jnp.concatenate([before, array, after], axis=dim)
    return array


def temporal_mix(padded, weights, count):
    result = jnp.zeros((count * padded.shape[1], padded.shape[2]), jnp.float32)
    for offset in range(3):
        window = padded[offset : offset + count].reshape(-1, padded.shape[2])
        result = result + jnp.dot(window, weights[offset], preferred_element_type=jnp.float32)
    return result


def absorb_keys(query_heads, channels, state_now, kv_pieces, piece_start):
    highest, denominator, accumulated = state_now
    joined = jnp.concatenate(kv_pieces, axis=0)
    key_heads = joined[:, :channels].reshape(-1, HEADS, HEAD_DIM)
    value_heads = joined[:, channels:].reshape(-1, HEADS, HEAD_DIM)
    scores = jnp.einsum(
        "qhd,khd->hqk", query_heads, key_heads, preferred_element_type=jnp.float32
    ) * HEAD_DIM ** (-0.5)
    raised = jnp.maximum(highest, jnp.max(scores, axis=-1))
    kept_frac = jnp.exp(highest - raised)
    exponent = jnp.exp(scores - raised[:, :, None])
    denominator = jnp.sum(exponent, axis=-1)
    contrib = jnp.einsum(
        "hqk,khd->qhd",
        exponent.astype(jnp.bfloat16),
        value_heads,
        preferred_element_type=jnp.float32,
    )
    accumulated = accumulated * jnp.repeat(kept_frac.T, HEAD_DIM, axis=1) + contrib.reshape(
        contrib.shape[0], -1
    )
    return (raised, denominator, accumulated)


def shards(frames, key_index, w_query, w_keyval, w_out, norm_gain, w_first, w_second):
    frame_count, row_count, channels = frames.shape
    flattened = frames.reshape(-1, channels)
    queries = jnp.dot(flattened, w_query, preferred_element_type=jnp.float32).astype(jnp.bfloat16)
    query_heads = queries.reshape(-1, HEADS, HEAD_DIM)
    query_total = queries.shape[0]
    owners = key_index // frame_count
    chosen = frames[key_index % frame_count].reshape(-1, channels)
    keyval = jnp.dot(chosen, w_keyval, preferred_element_type=jnp.float32).astype(jnp.bfloat16)
    own_parts = (keyval[:row_count], keyval[row_count:])
    initial = (
        jnp.full((HEADS, query_total), -1e30, jnp.float32),
        jnp.zeros((HEADS, query_total), jnp.float32),
        jnp.zeros((query_total, channels), jnp.float32),
    )
    absorb = partial(absorb_keys, query_heads, channels)
    spread_parts = []
    for key_slot in range(2):
        spread_parts.append(from_root(own_parts[key_slot], "frame", owners[key_slot]))
    final = absorb(
        initial,
        (
            lax.all_gather(spread_parts[0], "row", axis=0, tiled=True),
            lax.all_gather(spread_parts[1], "row", axis=0, tiled=True),
        ),
        jnp.int32(0),
    )
    highest, denominator, accumulated = final
    mixed = accumulated.reshape(query_total, HEADS, HEAD_DIM) / denominator.T[:, :, None]
    attended = mixed.reshape(query_total, channels).astype(jnp.bfloat16)
    residual = flattened.astype(jnp.float32) + jnp.dot(
        attended, w_out, preferred_element_type=jnp.float32
    )
    mean_square = jnp.mean(residual * residual, axis=-1, keepdims=True)
    normed = (residual * lax.rsqrt(mean_square + 1e-06) * norm_gain).astype(jnp.bfloat16)
    normed = normed.reshape(frame_count, row_count, channels)
    padded = extended(normed, (("frame", 0),), 1)
    hidden = jax.nn.silu(temporal_mix(padded, w_first, frame_count)).astype(jnp.bfloat16)
    hidden = hidden.reshape(frame_count, row_count, channels)
    padded = extended(hidden, (("frame", 0),), 1)
    second = temporal_mix(padded, w_second, frame_count)
    return (residual + second).astype(jnp.bfloat16).reshape(frame_count, row_count, channels)


def solution(mesh):
    return jax.shard_map(
        shards,
        mesh=mesh,
        in_specs=(P(("clips", "frame"), "row", None), P("clips"), P(), P(), P(), P(), P(), P()),
        out_specs=P(("clips", "frame"), "row", None),
        check_vma=False,
    )
```

profile of v0, /device:TPU:1, one launch (start us, length us, event | category | flops | bytes accessed | tf_op | source)
XLA Modules:
  0.0 162.4 jit_solution(13678371207064377667)
XLA Ops:
  6.5 0.0 copy-start
  6.5 0.8 and_select_fusion.1
  7.3 0.6 fusion.42
  9.2 1.6 gather_fusion
  10.8 0.0 copy-start.1
  10.8 0.0 copy-start.5
  10.8 0.7 convolution_convert_fusion
  11.5 0.9 slice_select_fusion
  12.4 0.0 all-reduce.3.cloned.1.call-update
  12.5 0.0 all-gather.3.cloned.1.call-start
  12.5 34.7 %all-reduce.3.cloned.1.call-done = (bf16[128,1280]{1,0:T(8,128)(2,1)}, bf16[128,1280]{1,0:T(8,128)(2,1)}) async-done(((bf16[128,1280]{1,0:T(8,128)(2,1)}, bf16[128,1280]{1,0:T(8,128)(2,1)}), (bf16[128,1280]{1,0:T(8,128)(2,1)}, bf16[128,1280]{1,0:T(8,128)(2,1)})) %all-reduce.3.cloned.1.call-update) | async-done | bytes 655376 | tf_op jit(solution)/shard_map/psum | solution.py:13
  47.2 0.0 all-gather.3.cloned.1.call-update
  47.2 0.0 all-gather.5.cloned.1.call-start
  47.3 0.7 all-gather.5.cloned.1.call-update
  48.0 0.5 convolution_convert_fusion.1
  48.4 0.9 copy.12
  49.4 32.9 %all-gather.3.cloned.1.call-done = bf16[512,1280]{1,0:T(8,128)(2,1)} async-done(((bf16[128,1280]{1,0:T(8,128)(2,1)}), bf16[512,1280]{1,0:T(8,128)(2,1)}) %all-gather.3.cloned.1.call-update) | async-done | bytes 1310736 | tf_op jit(solution)/shard_map/all_gather | solution.py:83
  82.2 2.5 %constant_dynamic-update-slice_fusion.1 = bf16[1024,1280]{1,0:T(8,128)(2,1)} fusion(bf16[512,1280]{1,0:T(8,128)(2,1)} %all-gather.3.cloned.1.call-done), kind=kLoop, calls=%fused_computation.54 | loop fusion | bytes 2621440
  84.7 30.8 %all-gather.5.cloned.1.call-done = bf16[512,1280]{1,0:T(8,128)(2,1)} async-done(((bf16[128,1280]{1,0:T(8,128)(2,1)}), bf16[512,1280]{1,0:T(8,128)(2,1)}) %all-gather.5.cloned.1.call-update) | async-done | bytes 1310736 | tf_op jit(solution)/shard_map/all_gather | solution.py:84
  115.5 2.5 %constant_dynamic-update-slice_fusion = bf16[1024,1280]{1,0:T(8,128)(2,1)} fusion(bf16[1024,1280]{1,0:T(8,128)(2,1)} %constant_dynamic-update-slice_fusion.1, bf16[512,1280]{1,0:T(8,128)(2,1)} %all-gather.5.cloned.1.call-done), kind=kLoop, calls=%fused_computation.53 | loop fusion | bytes 2621440 | tf_op jit(solution)/shard_map/concatenate | solution.py:39
  118.0 3.5 %fusion.41 = (bf16[1024,640]{1,0:T(8,128)(2,1)}, bf16[1024,640]{1,0:T(8,128)(2,1)}) fusion(bf16[1024,1280]{1,0:T(8,128)(2,1)} %constant_dynamic-update-slice_fusion), kind=kLoop, calls=%fused_computation.63 | loop fusion | bytes 5242880 | tf_op jit(solution)/shard_map/slice | solution.py:40
  121.5 1.6 copy.13
  123.1 2.5 %copy.14 = bf16[1024,640]{0,1:T(8,128)(2,1)} copy(bf16[1024,640]{1,0:T(8,128)(2,1)} %get-tuple-element.8) | data formatting | bytes 2621440 | tf_op jit(solution)/shard_map/slice | solution.py:41
  125.5 2.6 %multiply_reduce_fusion = (f32[10,256]{1,0:T(8,128)S(1)}, f32[10,256,1024]{2,1,0:T(8,128)S(1)}) fusion(bf16[256,10,64]{0,2,1:T(8,128)(2,1)} %bitcast.74, bf16[1024,10,64]{0,2,1:T(8,128)(2,1)S(1)} %bitcast.69), kind=kOutput, calls=%fused_computation.2 | convolution fusion | flops 340784640 | bytes 12134400 | tf_op jit(solution)/shard_map/qhd,khd->hqk/dot_general | solution.py:42
  128.2 2.1 %fusion = f32[10,256]{1,0:T(8,128)S(1)} fusion(f32[10,256,1024]{2,1,0:T(8,128)S(1)} %get-tuple-element.26, f32[10,256]{1,0:T(8,128)S(1)} %get-tuple-element.20), kind=kLoop, calls=%fused_computation.3 | loop fusion | flops 7861760 | bytes 10506240 | tf_op jit(solution)/shard_map/reduce_sum | solution.py:48
  130.2 0.0 copy-start.6
  130.3 0.0 copy-start.7
  130.3 2.3 %fusion.19 = bf16[256,10,64]{0,2,1:T(8,128)(2,1)S(1)} fusion(bf16[1024,10,64]{0,2,1:T(8,128)(2,1)S(1)} %bitcast.77, f32[10,256,1024]{2,1,0:T(8,128)S(1)} %get-tuple-element.26, f32[10,256]{1,0:T(8,128)S(1)} %get-tuple-element.20, f32[256,10]{0,1:T(8,128)S(1)} %bitcast.82, f32[256,10]{0,1:T(8,128)S(1)} %get-tuple-element.19), kind=kOutput, calls=%fused_computation.20 | convolution fusion | flops 343900160 | bytes 12154880 | tf_op jit(solution)/shard_map/hqk,khd->qhd/dot_general | solution.py:49
  132.6 0.0 copy-start.4
  132.6 0.6 multiply_reduce_fusion.1
  133.2 0.1 multiply_convert_fusion.1
  133.4 4.3 %collective-permute-start = (bf16[1,128,640]{2,1,0:T(8,128)(2,1)S(1)}, bf16[1,128,640]{2,1,0:T(8,128)(2,1)S(1)}, u32[]{:S(2)}, u32[]{:S(2)}) collective-permute-start(bf16[1,128,640]{2,1,0:T(8,128)(2,1)S(1)} %get-tuple-element.17), channel_id=1, source_target_pairs={{0,4},{4,8},{8,12},{1,5},{5,9},{9,13},{2,6},{6,10},{10,14},{3,7},{... | collective-permute-start | bytes 491528 | tf_op jit(solution)/shard_map/ppermute | solution.py:23
  137.7 1.9 %collective-permute-start.1 = (bf16[1,128,640]{2,1,0:T(8,128)(2,1)S(1)}, bf16[1,128,640]{2,1,0:T(8,128)(2,1)S(1)}, u32[]{:S(2)}, u32[]{:S(2)}) collective-permute-start(bf16[1,128,640]{2,1,0:T(8,128)(2,1)S(1)} %get-tuple-element.18), channel_id=1, source_target_pairs={{4,0},{8,4},{12,8},{5,1},{9,5},{13,9},{6,2},{10,6},{14,10},{7,3},{... | collective-permute-start | bytes 491528 | tf_op jit(solution)/shard_map/ppermute | solution.py:24
  139.6 0.5 fusion.29
  140.1 0.0 collective-permute-done
  140.1 4.2 %collective-permute-done.1 = bf16[1,128,640]{2,1,0:T(8,128)(2,1)S(1)} collective-permute-done((bf16[1,128,640]{2,1,0:T(8,128)(2,1)S(1)}, bf16[1,128,640]{2,1,0:T(8,128)(2,1)S(1)}, u32[]{:S(2)}, u32[]{:S(2)}) %collective-permute-start.1) | collective-permute-done | bytes 163872 | tf_op jit(solution)/shard_map/ppermute | solution.py:24
  144.3 0.1 pad_maximum_fusion.3
  144.4 0.5 fusion.27
  144.9 0.0 copy-start.2
  144.9 0.5 multiply_convert_fusion
  145.4 2.1 %collective-permute-start.2 = (bf16[1,128,640]{2,1,0:T(8,128)(2,1)S(1)}, bf16[1,128,640]{2,1,0:T(8,128)(2,1)S(1)}, u32[]{:S(2)}, u32[]{:S(2)}) collective-permute-start(bf16[1,128,640]{2,1,0:T(8,128)(2,1)S(1)} %get-tuple-element.13), channel_id=1, source_target_pairs={{0,4},{4,8},{8,12},{1,5},{5,9},{9,13},{2,6},{6,10},{10,14},{3,7},{... | collective-permute-start | bytes 491528 | tf_op jit(solution)/shard_map/ppermute | solution.py:23
  147.5 2.4 %collective-permute-start.3 = (bf16[1,128,640]{2,1,0:T(8,128)(2,1)S(1)}, bf16[1,128,640]{2,1,0:T(8,128)(2,1)S(1)}, u32[]{:S(2)}, u32[]{:S(2)}) collective-permute-start(bf16[1,128,640]{2,1,0:T(8,128)(2,1)S(1)} %get-tuple-element.14), channel_id=1, source_target_pairs={{4,0},{8,4},{12,8},{5,1},{9,5},{13,9},{6,2},{10,6},{14,10},{7,3},{... | collective-permute-start | bytes 491528 | tf_op jit(solution)/shard_map/ppermute | solution.py:24
  149.9 0.5 fusion.24
  150.4 0.0 collective-permute-done.2
  150.4 3.7 %collective-permute-done.3 = bf16[1,128,640]{2,1,0:T(8,128)(2,1)S(1)} collective-permute-done((bf16[1,128,640]{2,1,0:T(8,128)(2,1)S(1)}, bf16[1,128,640]{2,1,0:T(8,128)(2,1)S(1)}, u32[]{:S(2)}, u32[]{:S(2)}) %collective-permute-start.3) | collective-permute-done | bytes 163872 | tf_op jit(solution)/shard_map/ppermute | solution.py:24
  154.1 0.1 pad_maximum_fusion.1
  154.2 0.5 fusion.22
  154.7 1.2 fusion.15
  (15 shorter events, 0.1 us)
Async XLA Ops:
  6.5 4.3 %copy-start = (bf16[640,1280]{1,0:T(8,128)(2,1)S(1)}, bf16[640,1280]{1,0:T(8,128)(2,1)}, u32[]{:S(2)}) copy-start(bf16[640,1280]{1,0:T(8,128)(2,1)} %param.11) | copy-start | bytes 4915204
  6.5 40.7 %all-reduce.3.cloned.1.call-start = ((), (), s32[]{:S(2)}) async-start(), calls=%async_computation.2 | async-start | bytes 1310720 | tf_op jit(solution)/shard_map/psum | solution.py:13
  10.8 37.2 %copy-start.1 = (bf16[2,128,640]{2,1,0:T(8,128)(2,1)S(1)}, bf16[2,128,640]{2,1,0:T(8,128)(2,1)}, u32[]{:S(2)}) copy-start(bf16[2,128,640]{2,1,0:T(8,128)(2,1)} %param.8) | copy-start | bytes 983044
  10.8 37.2 %copy-start.5 = (bf16[640,640]{1,0:T(8,128)(2,1)S(1)}, bf16[640,640]{1,0:T(8,128)(2,1)}, u32[]{:S(2)}) copy-start(bf16[640,640]{1,0:T(8,128)(2,1)} %param.10) | copy-start | bytes 2457604
  12.5 69.8 %all-gather.3.cloned.1.call-start = ((), (), s32[]{:S(2)}) async-start(), calls=%async_computation | async-start | bytes 1638400 | tf_op jit(solution)/shard_map/all_gather | solution.py:83
  47.2 68.3 %all-gather.5.cloned.1.call-start = ((), (), s32[]{:S(2)}) async-start(), calls=%async_computation.1 | async-start | bytes 1638400 | tf_op jit(solution)/shard_map/all_gather | solution.py:84
  128.2 2.1 %copy-start.3 = (bf16[1024,640]{0,1:T(8,128)(2,1)S(1)}, bf16[1024,640]{0,1:T(8,128)(2,1)}, u32[]{:S(2)}) copy-start(bf16[1024,640]{0,1:T(8,128)(2,1)} %copy.14) | copy-start | bytes 3932164
  130.2 2.3 %copy-start.6 = (bf16[640,640]{1,0:T(8,128)(2,1)S(1)}, bf16[640,640]{1,0:T(8,128)(2,1)}, u32[]{:S(2)}) copy-start(bf16[640,640]{1,0:T(8,128)(2,1)} %param.12) | copy-start | bytes 2457604
  130.3 2.9 %copy-start.7 = (f32[640]{0:T(1024)S(1)}, f32[640]{0:T(1024)}, u32[]{:S(2)}) copy-start(f32[640]{0:T(1024)} %param.13) | copy-start | bytes 7684
  132.6 7.1 %copy-start.4 = (bf16[3,640,640]{2,1,0:T(8,128)(2,1)S(1)}, bf16[3,640,640]{2,1,0:T(8,128)(2,1)}, u32[]{:S(2)}) copy-start(bf16[3,640,640]{2,1,0:T(8,128)(2,1)} %param.14) | copy-start | bytes 7372804
  133.4 6.7 %collective-permute-start = (bf16[1,128,640]{2,1,0:T(8,128)(2,1)S(1)}, bf16[1,128,640]{2,1,0:T(8,128)(2,1)S(1)}, u32[]{:S(2)}, u32[]{:S(2)}) collective-permute-start(bf16[1,128,640]{2,1,0:T(8,128)(2,1)S(1)} %get-tuple-element.17), channel_id=1, source_target_pairs={{0,4},{4,8},{8,12},{1,5},{5,9},{9,13},{2,6},{6,10},{10,14},{3,7},{... | collective-permute-start | bytes 491528 | tf_op jit(solution)/shard_map/ppermute | solution.py:23
  137.7 6.6 %collective-permute-start.1 = (bf16[1,128,640]{2,1,0:T(8,128)(2,1)S(1)}, bf16[1,128,640]{2,1,0:T(8,128)(2,1)S(1)}, u32[]{:S(2)}, u32[]{:S(2)}) collective-permute-start(bf16[1,128,640]{2,1,0:T(8,128)(2,1)S(1)} %get-tuple-element.18), channel_id=1, source_target_pairs={{4,0},{8,4},{12,8},{5,1},{9,5},{13,9},{6,2},{10,6},{14,10},{7,3},{... | collective-permute-start | bytes 491528 | tf_op jit(solution)/shard_map/ppermute | solution.py:24
  144.9 5.1 %copy-start.2 = (bf16[3,640,640]{2,1,0:T(8,128)(2,1)S(1)}, bf16[3,640,640]{2,1,0:T(8,128)(2,1)}, u32[]{:S(2)}) copy-start(bf16[3,640,640]{2,1,0:T(8,128)(2,1)} %param.15) | copy-start | bytes 7372804
  145.4 5.0 %collective-permute-start.2 = (bf16[1,128,640]{2,1,0:T(8,128)(2,1)S(1)}, bf16[1,128,640]{2,1,0:T(8,128)(2,1)S(1)}, u32[]{:S(2)}, u32[]{:S(2)}) collective-permute-start(bf16[1,128,640]{2,1,0:T(8,128)(2,1)S(1)} %get-tuple-element.13), channel_id=1, source_target_pairs={{0,4},{4,8},{8,12},{1,5},{5,9},{9,13},{2,6},{6,10},{10,14},{3,7},{... | collective-permute-start | bytes 491528 | tf_op jit(solution)/shard_map/ppermute | solution.py:23
  147.5 6.6 %collective-permute-start.3 = (bf16[1,128,640]{2,1,0:T(8,128)(2,1)S(1)}, bf16[1,128,640]{2,1,0:T(8,128)(2,1)S(1)}, u32[]{:S(2)}, u32[]{:S(2)}) collective-permute-start(bf16[1,128,640]{2,1,0:T(8,128)(2,1)S(1)} %get-tuple-element.14), channel_id=1, source_target_pairs={{4,0},{8,4},{12,8},{5,1},{9,5},{13,9},{6,2},{10,6},{14,10},{7,3},{... | collective-permute-start | bytes 491528 | tf_op jit(solution)/shard_map/ppermute | solution.py:24
Sparse Core Ops, SparseCore 0:
  12.6 34.5 all-reduce.2
  48.8 33.4 all-gather.2
  83.8 31.6 all-gather.4
where the time goes:
time: 163 us; the launch traced here: 162 us
  waiting for transfers between devices  107 us (66%)
  local copies, waits for them, and re-layouts  15.6 us (10%)
  between operations  14.7 us (9%)
  starting transfers between devices  10.8 us (7%)
  matrix products  10.2 us (6%)
  other arithmetic  4.05 us (2%)
    psum x1, waiting for transfers between devices, from_root(): return lax.psum(kept, axis)  34.7 us
    all_gather x1, waiting for transfers between devices, shards(): lax.all_gather(spread_parts[0], 'row', axis=0, tiled=True)  32.9 us
    all_gather x1, waiting for transfers between devices, shards(): lax.all_gather(spread_parts[1], 'row', axis=0, tiled=True)  30.8 us
    ppermute x2, waiting for transfers between devices, extended(): after = lax.ppermute(first, axis, down)  7.96 us
    ppermute x2, starting transfers between devices, extended(): before = lax.ppermute(last, axis, up)  6.37 us
    slice x2, local copies, waits for them, and re-layouts, absorb_keys(): key_heads = joined[:, :channels].reshape(-1, HEADS, HEAD_DIM)  5.06 us
    ppermute x2, starting transfers between devices, extended(): after = lax.ppermute(first, axis, down)  4.33 us
    dot_general x6, matrix products, temporal_mix(): jnp.dot(window, weights[offset], preferred_element_type=jnp.float32)  3.53 us
  transfers between devices with their start and end apart: 7, of which 5 were waited for; matrix products, arithmetic and copies ran while one was open for 3% of the time, Pallas kernels for 0%

commit v1 on v0

--- a/solution.py
+++ b/solution.py
@@ -1,3 +1,4 @@
+import functools
 from functools import partial
 import jax
 import jax.numpy as jnp
@@ -6,6 +7,43 @@
 
 HEADS = 10
 HEAD_DIM = 64
+
+
+def choose_sums_all_in(local, k_dim):
+    current_arr, block_out, x_new = (
+        lax.axis_size("row"),
+        lax.axis_index("row"),
+        local.shape[k_dim],
+    )
+    res = lax.dynamic_update_slice_in_dim(
+        jnp.zeros(
+            [k * current_arr if no == k_dim else k for no, k in enumerate(local.shape)], local.dtype
+        ),
+        local,
+        block_out * x_new,
+        axis=k_dim,
+    )
+    piece_now = p_next = local
+    for b in range(1, current_arr // 2 + 1):
+        piece_now = lax.ppermute(
+            piece_now, "row", list(map(lambda no: (no, (no + 1) % current_arr), range(current_arr)))
+        )
+        res = lax.dynamic_update_slice_in_dim(
+            res, piece_now, (block_out - b) % current_arr * x_new, axis=k_dim
+        )
+        if 2 * b < current_arr:
+            p_next = lax.ppermute(
+                p_next,
+                "row",
+                perm=list(map(lambda no: (no, (no - 1) % current_arr), range(current_arr))),
+            )
+            res = lax.dynamic_update_slice_in_dim(
+                res, p_next, (block_out + b) % current_arr * x_new, axis=k_dim
+            )
+    return res
+
+
+pass_the_flows = functools.partial(choose_sums_all_in, k_dim=0)
 
 
 def from_root(value, axis, source):
@@ -80,7 +118,7 @@
     final = absorb(
         initial,
         (
-            lax.all_gather(spread_parts[0], "row", axis=0, tiled=True),
+            pass_the_flows(spread_parts[0]),
             lax.all_gather(spread_parts[1], "row", axis=0, tiled=True),
         ),
         jnp.int32(0),

time: 163 us -> 138 us (0.85)
  waiting for transfers between devices: 107 us -> 82.9 us
  local copies, waits for them, and re-layouts: 15.6 us -> 9.45 us
  other arithmetic: 4.05 us -> 7 us
  starting transfers between devices: 10.8 us -> 13.2 us
    all_gather x1 -> x0, waiting for transfers between devices: 32.9 us -> none  [shards(): lax.all_gather(spread_parts[0], 'row', axis=0, tiled=True)]
    ppermute x0 -> x3, waiting for transfers between devices: none -> 26.2 us  [the longest x1 22.5 us: choose_sums_all_in(): lax.ppermute(p_next, 'row', perm=list(map(lambda no: (no, (no - 1) % curr...]
    all_gather x1, waiting for transfers between devices: 30.8 us -> 14 us  [shards(): lax.all_gather(spread_parts[1], 'row', axis=0, tiled=True)]
    ppermute x0 -> x3, starting transfers between devices: none -> 3.62 us  [the longest x1 1.87 us: choose_sums_all_in(): lax.ppermute(p_next, 'row', perm=list(map(lambda no: (no, (no - 1) % curr...]
    slice x2 -> x1, local copies, waits for them, and re-layouts: 5.06 us -> 1.6 us  [absorb_keys(): key_heads = joined[:, :channels].reshape(-1, HEADS, HEAD_DIM)]
    concatenate x0 -> x1, other arithmetic: none -> 2.98 us  [absorb_keys(): joined = jnp.concatenate(kv_pieces, axis=0)]
    unnamed x17 -> x16, local copies, waits for them, and re-layouts: 2.52 us -> 0.05 us
    concatenate x1 -> x0, local copies, waits for them, and re-layouts: 2.46 us -> none  [absorb_keys(): joined = jnp.concatenate(kv_pieces, axis=0)]
  transfers between devices with their start and end apart: 7 -> 9, of which waited for: 5 -> 6; matrix products, arithmetic and copies ran while one was open for 3% -> 3% of each run, Pallas kernels for 0% -> 0%
where the time goes in v1:
time: 138 us
  waiting for transfers between devices  82.9 us (60%)
  between operations  15 us (11%)
  starting transfers between devices  13.2 us (10%)
  matrix products  10.2 us (7%)
  local copies, waits for them, and re-layouts  9.45 us (7%)
  other arithmetic  7 us (5%)
    psum x1, waiting for transfers between devices, from_root(): return lax.psum(kept, axis)  34.7 us
    ppermute x1, waiting for transfers between devices, choose_sums_all_in(): lax.ppermute(p_next, 'row', perm=list(map(lambda no: (no, (no - 1) % curr...  22.5 us
    all_gather x1, waiting for transfers between devices, shards(): lax.all_gather(spread_parts[1], 'row', axis=0, tiled=True)  14 us
    ppermute x2, waiting for transfers between devices, extended(): after = lax.ppermute(first, axis, down)  7.96 us
    ppermute x2, starting transfers between devices, extended(): before = lax.ppermute(last, axis, up)  5.2 us
    ppermute x2, starting transfers between devices, extended(): after = lax.ppermute(first, axis, down)  4.33 us
    ppermute x2, waiting for transfers between devices, choose_sums_all_in(): lax.ppermute(piece_now, 'row', list(map(lambda no: (no, (no + 1) % curren...  3.76 us
    dot_general x6, matrix products, temporal_mix(): jnp.dot(window, weights[offset], preferred_element_type=jnp.float32)  3.53 us
  transfers between devices with their start and end apart: 9, of which 6 were waited for; matrix products, arithmetic and copies ran while one was open for 3% of the time, Pallas kernels for 0%

profile of v1, /device:TPU:1, one launch (start us, length us, event | category | flops | bytes accessed | tf_op | source)
XLA Modules:
  0.0 137.8 jit_solution(853758454877228658)
XLA Ops:
  6.5 0.8 and_select_fusion.1
  7.3 0.6 fusion.42
  9.2 1.6 %gather_fusion = bf16[2,128,640]{2,1,0:T(8,128)(2,1)S(1)} fusion(bf16[2,128,640]{2,1,0:T(8,128)(2,1)} %param.8, s32[1024]{0:T(1024)S(1)} %pad_clamp_fusion), kind=kCustom, calls=%fused_computation | custom fusion | bytes 655368 | tf_op jit(solution)/shard_map/gather | solution.py:106
  10.8 0.0 copy-start.1
  10.9 0.0 copy-start.5
  10.9 0.7 convolution_convert_fusion
  11.6 0.9 slice_select_fusion.1
  12.4 0.0 all-reduce.3.cloned.1.call-update
  12.5 0.0 all-gather.2.cloned.1.call-start
  12.5 34.7 %all-reduce.3.cloned.1.call-done = (bf16[128,1280]{1,0:T(8,128)(2,1)}, bf16[128,1280]{1,0:T(8,128)(2,1)}) async-done(((bf16[128,1280]{1,0:T(8,128)(2,1)}, bf16[128,1280]{1,0:T(8,128)(2,1)}), (bf16[128,1280]{1,0:T(8,128)(2,1)}, bf16[128,1280]{1,0:T(8,128)(2,1)})) %all-reduce.3.cloned.1.call-update) | async-done | bytes 655376 | tf_op jit(solution)/shard_map/psum | solution.py:51
  47.2 0.0 all-gather.2.cloned.1.call-update
  47.2 1.7 %collective-permute-start = (bf16[128,1280]{1,0:T(8,128)(2,1)}, bf16[128,1280]{1,0:T(8,128)(2,1)}, u32[]{:S(2)}, u32[]{:S(2)}) collective-permute-start(bf16[128,1280]{1,0:T(8,128)(2,1)} %get-tuple-element.6), channel_id=1, source_target_pairs={{0,1},{1,2},{2,3},{3,0},{4,5},{5,6},{6,7},{7,4},{8,9},{9,10},{10,1... | collective-permute-start | bytes 983048 | tf_op jit(solution)/shard_map/ppermute | solution.py:28
  49.0 0.5 convolution_convert_fusion.1
  49.5 0.9 copy.12
  50.4 1.9 %collective-permute-start.1 = (bf16[128,1280]{1,0:T(8,128)(2,1)}, bf16[128,1280]{1,0:T(8,128)(2,1)S(1)}, u32[]{:S(2)}, u32[]{:S(2)}) collective-permute-start(bf16[128,1280]{1,0:T(8,128)(2,1)} %get-tuple-element.6), channel_id=1, source_target_pairs={{0,3},{1,0},{2,1},{3,2},{4,7},{5,4},{6,5},{7,6},{8,11},{9,8},{10,9... | collective-permute-start | bytes 983048 | tf_op jit(solution)/shard_map/ppermute | solution.py:35
  52.3 0.1 broadcast_in_dim.25
  52.4 1.0 constant_dynamic-update-slice_fusion.3
  53.4 3.8 %collective-permute-done = bf16[128,1280]{1,0:T(8,128)(2,1)} collective-permute-done((bf16[128,1280]{1,0:T(8,128)(2,1)}, bf16[128,1280]{1,0:T(8,128)(2,1)}, u32[]{:S(2)}, u32[]{:S(2)}) %collective-permute-start) | collective-permute-done | bytes 327712 | tf_op jit(solution)/shard_map/ppermute | solution.py:28
  57.1 1.0 constant_dynamic-update-slice_fusion.2
  58.2 22.5 %collective-permute-done.1 = bf16[128,1280]{1,0:T(8,128)(2,1)S(1)} collective-permute-done((bf16[128,1280]{1,0:T(8,128)(2,1)}, bf16[128,1280]{1,0:T(8,128)(2,1)S(1)}, u32[]{:S(2)}, u32[]{:S(2)}) %collective-permute-start.1) | collective-permute-done | bytes 327712 | tf_op jit(solution)/shard_map/ppermute | solution.py:35
  80.7 14.0 %all-gather.2.cloned.1.call-done = bf16[512,1280]{1,0:T(8,128)(2,1)} async-done(((bf16[128,1280]{1,0:T(8,128)(2,1)}), bf16[512,1280]{1,0:T(8,128)(2,1)}) %all-gather.2.cloned.1.call-update) | async-done | bytes 1310736 | tf_op jit(solution)/shard_map/all_gather | solution.py:122
  94.7 3.0 %fusion.6 = (bf16[1024,640]{1,0:T(8,128)(2,1)}, bf16[1024,640]{1,0:T(8,128)(2,1)}) fusion(bf16[512,1280]{1,0:T(8,128)(2,1)S(1)} %constant_dynamic-update-slice_fusion, bf16[512,1280]{1,0:T(8,128)(2,1)} %all-gather.2.cloned.1.call-done), kind=kLoop, calls=%fused_computation.11 | loop fusion | flops 5242880 | bytes 5242880 | tf_op jit(solution)/shard_map/concatenate | solution.py:77
  97.7 1.6 %copy.13 = bf16[1024,640]{0,1:T(8,128)(2,1)S(1)} copy(bf16[1024,640]{1,0:T(8,128)(2,1)} %get-tuple-element.7) | data formatting | bytes 2621440 | tf_op jit(solution)/shard_map/slice | solution.py:78
  99.3 2.5 %copy.14 = bf16[1024,640]{0,1:T(8,128)(2,1)} copy(bf16[1024,640]{1,0:T(8,128)(2,1)} %get-tuple-element.8) | data formatting | bytes 2621440 | tf_op jit(solution)/shard_map/slice | solution.py:79
  101.8 2.6 %multiply_reduce_fusion = (f32[10,256]{1,0:T(8,128)S(1)}, f32[10,256,1024]{2,1,0:T(8,128)S(1)}) fusion(bf16[256,10,64]{0,2,1:T(8,128)(2,1)} %bitcast.74, bf16[1024,10,64]{0,2,1:T(8,128)(2,1)S(1)} %bitcast.69), kind=kOutput, calls=%fused_computation.2 | convolution fusion | flops 340784640 | bytes 12134400 | tf_op jit(solution)/shard_map/qhd,khd->hqk/dot_general | solution.py:80
  104.4 2.1 %fusion = f32[10,256]{1,0:T(8,128)S(1)} fusion(f32[10,256,1024]{2,1,0:T(8,128)S(1)} %get-tuple-element.26, f32[10,256]{1,0:T(8,128)S(1)} %get-tuple-element.20), kind=kLoop, calls=%fused_computation.3 | loop fusion | flops 7861760 | bytes 10506240 | tf_op jit(solution)/shard_map/reduce_sum | solution.py:86
  106.5 0.0 copy-start.6
  106.5 0.0 copy-start.7
  106.5 2.3 %fusion.20 = bf16[256,10,64]{0,2,1:T(8,128)(2,1)S(1)} fusion(bf16[1024,10,64]{0,2,1:T(8,128)(2,1)S(1)} %bitcast.77, f32[10,256,1024]{2,1,0:T(8,128)S(1)} %get-tuple-element.26, f32[10,256]{1,0:T(8,128)S(1)} %get-tuple-element.20, f32[256,10]{0,1:T(8,128)S(1)} %bitcast.82, f32[256,10]{0,1:T(8,128)S(1)} %get-tuple-element.19), kind=kOutput, calls=%fused_computation.24 | convolution fusion | flops 343900160 | bytes 12154880 | tf_op jit(solution)/shard_map/hqk,khd->qhd/dot_general | solution.py:87
  108.8 0.0 copy-start.4
  108.9 0.6 multiply_reduce_fusion.1
  109.5 0.1 multiply_convert_fusion.1
  109.6 3.1 %collective-permute-start.3 = (bf16[1,128,640]{2,1,0:T(8,128)(2,1)S(1)}, bf16[1,128,640]{2,1,0:T(8,128)(2,1)S(1)}, u32[]{:S(2)}, u32[]{:S(2)}) collective-permute-start(bf16[1,128,640]{2,1,0:T(8,128)(2,1)S(1)} %get-tuple-element.17), channel_id=1, source_target_pairs={{0,4},{4,8},{8,12},{1,5},{5,9},{9,13},{2,6},{6,10},{10,14},{3,7},{... | collective-permute-start | bytes 491528 | tf_op jit(solution)/shard_map/ppermute | solution.py:61
  112.8 1.9 %collective-permute-start.4 = (bf16[1,128,640]{2,1,0:T(8,128)(2,1)S(1)}, bf16[1,128,640]{2,1,0:T(8,128)(2,1)S(1)}, u32[]{:S(2)}, u32[]{:S(2)}) collective-permute-start(bf16[1,128,640]{2,1,0:T(8,128)(2,1)S(1)} %get-tuple-element.18), channel_id=1, source_target_pairs={{4,0},{8,4},{12,8},{5,1},{9,5},{13,9},{6,2},{10,6},{14,10},{7,3},{... | collective-permute-start | bytes 491528 | tf_op jit(solution)/shard_map/ppermute | solution.py:62
  114.7 0.5 fusion.30
  115.2 0.0 collective-permute-done.3
  115.2 4.2 %collective-permute-done.4 = bf16[1,128,640]{2,1,0:T(8,128)(2,1)S(1)} collective-permute-done((bf16[1,128,640]{2,1,0:T(8,128)(2,1)S(1)}, bf16[1,128,640]{2,1,0:T(8,128)(2,1)S(1)}, u32[]{:S(2)}, u32[]{:S(2)}) %collective-permute-start.4) | collective-permute-done | bytes 163872 | tf_op jit(solution)/shard_map/ppermute | solution.py:62
  119.4 0.1 pad_maximum_fusion.4
  119.5 0.5 fusion.28
  120.0 0.0 copy-start.2
  120.0 0.5 multiply_convert_fusion
  120.5 2.1 %collective-permute-start.5 = (bf16[1,128,640]{2,1,0:T(8,128)(2,1)S(1)}, bf16[1,128,640]{2,1,0:T(8,128)(2,1)S(1)}, u32[]{:S(2)}, u32[]{:S(2)}) collective-permute-start(bf16[1,128,640]{2,1,0:T(8,128)(2,1)S(1)} %get-tuple-element.13), channel_id=1, source_target_pairs={{0,4},{4,8},{8,12},{1,5},{5,9},{9,13},{2,6},{6,10},{10,14},{3,7},{... | collective-permute-start | bytes 491528 | tf_op jit(solution)/shard_map/ppermute | solution.py:61
  122.6 2.4 %collective-permute-start.6 = (bf16[1,128,640]{2,1,0:T(8,128)(2,1)S(1)}, bf16[1,128,640]{2,1,0:T(8,128)(2,1)S(1)}, u32[]{:S(2)}, u32[]{:S(2)}) collective-permute-start(bf16[1,128,640]{2,1,0:T(8,128)(2,1)S(1)} %get-tuple-element.14), channel_id=1, source_target_pairs={{4,0},{8,4},{12,8},{5,1},{9,5},{13,9},{6,2},{10,6},{14,10},{7,3},{... | collective-permute-start | bytes 491528 | tf_op jit(solution)/shard_map/ppermute | solution.py:62
  125.0 0.5 fusion.25
  125.5 3.7 %collective-permute-done.6 = bf16[1,128,640]{2,1,0:T(8,128)(2,1)S(1)} collective-permute-done((bf16[1,128,640]{2,1,0:T(8,128)(2,1)S(1)}, bf16[1,128,640]{2,1,0:T(8,128)(2,1)S(1)}, u32[]{:S(2)}, u32[]{:S(2)}) %collective-permute-start.6) | collective-permute-done | bytes 163872 | tf_op jit(solution)/shard_map/ppermute | solution.py:62
  129.2 0.1 pad_maximum_fusion.2
  129.3 0.5 fusion.23
  129.8 1.2 fusion.16
  (21 shorter events, 0.2 us)
Async XLA Ops:
  6.5 4.3 %copy-start = (bf16[640,1280]{1,0:T(8,128)(2,1)S(1)}, bf16[640,1280]{1,0:T(8,128)(2,1)}, u32[]{:S(2)}) copy-start(bf16[640,1280]{1,0:T(8,128)(2,1)} %param.11) | copy-start | bytes 4915204
  6.5 40.7 %all-reduce.3.cloned.1.call-start = ((), (), s32[]{:S(2)}) async-start(), calls=%async_computation.1 | async-start | bytes 1310720 | tf_op jit(solution)/shard_map/psum | solution.py:51
  10.8 38.1 %copy-start.1 = (bf16[2,128,640]{2,1,0:T(8,128)(2,1)S(1)}, bf16[2,128,640]{2,1,0:T(8,128)(2,1)}, u32[]{:S(2)}) copy-start(bf16[2,128,640]{2,1,0:T(8,128)(2,1)} %param.8) | copy-start | bytes 983044
  10.9 38.1 %copy-start.5 = (bf16[640,640]{1,0:T(8,128)(2,1)S(1)}, bf16[640,640]{1,0:T(8,128)(2,1)}, u32[]{:S(2)}) copy-start(bf16[640,640]{1,0:T(8,128)(2,1)} %param.10) | copy-start | bytes 2457604
  12.5 82.3 %all-gather.2.cloned.1.call-start = ((), (), s32[]{:S(2)}) async-start(), calls=%async_computation | async-start | bytes 1638400 | tf_op jit(solution)/shard_map/all_gather | solution.py:122
  47.2 9.9 %collective-permute-start = (bf16[128,1280]{1,0:T(8,128)(2,1)}, bf16[128,1280]{1,0:T(8,128)(2,1)}, u32[]{:S(2)}, u32[]{:S(2)}) collective-permute-start(bf16[128,1280]{1,0:T(8,128)(2,1)} %get-tuple-element.6), channel_id=1, source_target_pairs={{0,1},{1,2},{2,3},{3,0},{4,5},{5,6},{6,7},{7,4},{8,9},{9,10},{10,1... | collective-permute-start | bytes 983048 | tf_op jit(solution)/shard_map/ppermute | solution.py:28
  50.4 30.2 %collective-permute-start.1 = (bf16[128,1280]{1,0:T(8,128)(2,1)}, bf16[128,1280]{1,0:T(8,128)(2,1)S(1)}, u32[]{:S(2)}, u32[]{:S(2)}) collective-permute-start(bf16[128,1280]{1,0:T(8,128)(2,1)} %get-tuple-element.6), channel_id=1, source_target_pairs={{0,3},{1,0},{2,1},{3,2},{4,7},{5,4},{6,5},{7,6},{8,11},{9,8},{10,9... | collective-permute-start | bytes 983048 | tf_op jit(solution)/shard_map/ppermute | solution.py:35
  57.1 23.5 %collective-permute-start.2 = (bf16[128,1280]{1,0:T(8,128)(2,1)}, bf16[128,1280]{1,0:T(8,128)(2,1)S(1)}, u32[]{:S(2)}, u32[]{:S(2)}) collective-permute-start(bf16[128,1280]{1,0:T(8,128)(2,1)} %collective-permute-done), channel_id=1, source_target_pairs={{0,1},{1,2},{2,3},{3,0},{4,5},{5,6},{6,7},{7,4},{8,9},{9,10},{10,1... | collective-permute-start | bytes 983048 | tf_op jit(solution)/shard_map/ppermute | solution.py:28
  104.4 2.1 %copy-start.3 = (bf16[1024,640]{0,1:T(8,128)(2,1)S(1)}, bf16[1024,640]{0,1:T(8,128)(2,1)}, u32[]{:S(2)}) copy-start(bf16[1024,640]{0,1:T(8,128)(2,1)} %copy.14) | copy-start | bytes 3932164
  106.5 2.4 %copy-start.6 = (bf16[640,640]{1,0:T(8,128)(2,1)S(1)}, bf16[640,640]{1,0:T(8,128)(2,1)}, u32[]{:S(2)}) copy-start(bf16[640,640]{1,0:T(8,128)(2,1)} %param.12) | copy-start | bytes 2457604
  106.5 2.9 %copy-start.7 = (f32[640]{0:T(1024)S(1)}, f32[640]{0:T(1024)}, u32[]{:S(2)}) copy-start(f32[640]{0:T(1024)} %param.13) | copy-start | bytes 7684
  108.8 5.9 %copy-start.4 = (bf16[3,640,640]{2,1,0:T(8,128)(2,1)S(1)}, bf16[3,640,640]{2,1,0:T(8,128)(2,1)}, u32[]{:S(2)}) copy-start(bf16[3,640,640]{2,1,0:T(8,128)(2,1)} %param.14) | copy-start | bytes 7372804
  109.6 5.6 %collective-permute-start.3 = (bf16[1,128,640]{2,1,0:T(8,128)(2,1)S(1)}, bf16[1,128,640]{2,1,0:T(8,128)(2,1)S(1)}, u32[]{:S(2)}, u32[]{:S(2)}) collective-permute-start(bf16[1,128,640]{2,1,0:T(8,128)(2,1)S(1)} %get-tuple-element.17), channel_id=1, source_target_pairs={{0,4},{4,8},{8,12},{1,5},{5,9},{9,13},{2,6},{6,10},{10,14},{3,7},{... | collective-permute-start | bytes 491528 | tf_op jit(solution)/shard_map/ppermute | solution.py:61
  112.8 6.6 %collective-permute-start.4 = (bf16[1,128,640]{2,1,0:T(8,128)(2,1)S(1)}, bf16[1,128,640]{2,1,0:T(8,128)(2,1)S(1)}, u32[]{:S(2)}, u32[]{:S(2)}) collective-permute-start(bf16[1,128,640]{2,1,0:T(8,128)(2,1)S(1)} %get-tuple-element.18), channel_id=1, source_target_pairs={{4,0},{8,4},{12,8},{5,1},{9,5},{13,9},{6,2},{10,6},{14,10},{7,3},{... | collective-permute-start | bytes 491528 | tf_op jit(solution)/shard_map/ppermute | solution.py:62
  120.0 5.1 %copy-start.2 = (bf16[3,640,640]{2,1,0:T(8,128)(2,1)S(1)}, bf16[3,640,640]{2,1,0:T(8,128)(2,1)}, u32[]{:S(2)}) copy-start(bf16[3,640,640]{2,1,0:T(8,128)(2,1)} %param.15) | copy-start | bytes 7372804
  120.5 5.0 %collective-permute-start.5 = (bf16[1,128,640]{2,1,0:T(8,128)(2,1)S(1)}, bf16[1,128,640]{2,1,0:T(8,128)(2,1)S(1)}, u32[]{:S(2)}, u32[]{:S(2)}) collective-permute-start(bf16[1,128,640]{2,1,0:T(8,128)(2,1)S(1)} %get-tuple-element.13), channel_id=1, source_target_pairs={{0,4},{4,8},{8,12},{1,5},{5,9},{9,13},{2,6},{6,10},{10,14},{3,7},{... | collective-permute-start | bytes 491528 | tf_op jit(solution)/shard_map/ppermute | solution.py:61
  122.6 6.6 %collective-permute-start.6 = (bf16[1,128,640]{2,1,0:T(8,128)(2,1)S(1)}, bf16[1,128,640]{2,1,0:T(8,128)(2,1)S(1)}, u32[]{:S(2)}, u32[]{:S(2)}) collective-permute-start(bf16[1,128,640]{2,1,0:T(8,128)(2,1)S(1)} %get-tuple-element.14), channel_id=1, source_target_pairs={{4,0},{8,4},{12,8},{5,1},{9,5},{13,9},{6,2},{10,6},{14,10},{7,3},{... | collective-permute-start | bytes 491528 | tf_op jit(solution)/shard_map/ppermute | solution.py:62
Sparse Core Ops, SparseCore 0:
  12.6 34.5 all-reduce.2
  48.8 45.9 all-gather.1
